TPU v7x, 512 devices: a whole 4x8x8 slice. The times are simulated.
512 devices in a mesh: row: 64 (over y, x, core), col: 8 (over z).
Axes of the slice: x: 4, y: 8, z: 8, core: 2. Of those that a mesh axis runs over, the one named last changes fastest.
Arguments:
- panel_cols: float32 [16384, 256], P('row'), may hold values from -60 to 60, as said below
- affinity: float32 [16384, 16384], P('row', 'col'), may hold values from -8 to 8, as said below
Outputs:
- updated: float32 [16384, 16384], P('row', 'col')
- band_block: float32 [256, 256], replicated
Inputs may be any that keep to these rules, and one draw needn't show every extreme that they name: affinity holds a symmetric matrix in the stored column order of the steps. panel_cols has full column rank.
All inputs are finite; a program needn't handle non-finite values.
Results may differ from a plain program's by a relative error of at most 0.000071.
Values sent between devices are 32-bit elements; how exact they have to be, the bound alone decides.
No kernel may reach another device: no remote copies, remote signals or barrier semaphores. Data moves between devices by JAX's collectives and lax.ppermute only.
A program may use at most 64 MiB of HBM per device.

v0:
```python
import jax
import jax.numpy as jnp
from jax import lax
from jax.sharding import PartitionSpec as P


def shards(panel_cols, affinity):
    high = lax.Precision.HIGHEST
    local_rows = panel_cols.shape[0]
    piece_rows = local_rows // lax.axis_size("col")
    col_place = lax.axis_index("col")
    gram_sum = lax.psum(jnp.dot(panel_cols.T, panel_cols, precision=high), "row")
    lower_factor = jnp.linalg.cholesky(gram_sum)
    ortho_basis = jax.scipy.linalg.solve_triangular(lower_factor, panel_cols.T, lower=True).T
    own_basis = lax.dynamic_slice_in_dim(ortho_basis, col_place * piece_rows, piece_rows, 0)
    arrived = lax.all_gather(own_basis, "row", axis=0, tiled=True)
    partial_sum = jnp.dot(affinity, arrived, precision=high)
    partial_sum, basis_cols = (partial_sum, arrived)
    moment = lax.psum(partial_sum, "col")
    band_block = lax.psum(jnp.dot(ortho_basis.T, moment, precision=high), "row")
    corrected = moment - 0.5 * jnp.dot(ortho_basis, band_block, precision=high)
    own_corrected = lax.dynamic_slice_in_dim(corrected, col_place * piece_rows, piece_rows, 0)
    update_cols = lax.all_gather(own_corrected, "row", axis=0, tiled=True)
    updated = affinity - jnp.dot(ortho_basis, update_cols.T, precision=high)
    updated = updated - jnp.dot(corrected, basis_cols.T, precision=high)
    return (updated, band_block)


def solution(mesh):
    placed = (P("row", None), P("row", "col"))
    return jax.shard_map(
        shards, mesh=mesh, in_specs=placed, out_specs=(P("row", "col"), P()), check_vma=False
    )
```

profile of v0, /device:TPU:1, one launch (start us, length us, event | category | flops | bytes accessed | tf_op | source)
XLA Modules:
  0.0 722.9 jit_solution(2886932835697183772)
XLA Ops:
  7.2 2.3 fusion.16
  9.6 196.8 %all-reduce.5.cloned.1.call-done = f32[256,256]{0,1:T(8,128)} async-done(((f32[256,256]{0,1:T(8,128)}), f32[256,256]{0,1:T(8,128)}) %all-reduce.5.cloned.1.call-update) | async-done | bytes 262160 | tf_op jit(solution)/shard_map/psum | solution.py:12
  206.4 1.1 copy.8
  207.5 1.0 fusion.1
  208.5 11.7 %cholesky.50 = f32[128,128]{1,0:T(8,128)S(1)} custom-call(f32[128,128]{1,0:T(8,128)S(1)} %cholesky.118), custom_call_target="Cholesky" | custom-call | tf_op jit(solution)/shard_map/jit(cholesky)/cholesky | solution.py:13
  220.3 9.8 %custom-call.15 = f32[1,128,128]{1,2,0:T(8,128)S(1)} custom-call(f32[1,128,128]{2,1,0:T(8,128)S(1)} %get-tuple-element.23), custom_call_target="InvertDiagBlocksLowerTriangular" | custom-call | tf_op jit(solution)/shard_map/jit(cholesky)/cholesky | solution.py:13
  230.6 11.7 %cholesky.105 = f32[128,128]{1,0:T(8,128)S(1)} custom-call(f32[128,128]{1,0:T(8,128)S(1)} %convolution_subtract_fusion.3), custom_call_target="Cholesky" | custom-call | tf_op jit(solution)/shard_map/jit(cholesky)/cholesky | solution.py:13
  242.3 0.7 compare_reduce_fusion
  244.4 4.1 while.1
  245.1 1.4 bitcast_dynamic-update-slice_fusion.2
  247.1 1.4 bitcast_dynamic-update-slice_fusion.2
  248.5 19.7 %custom-call.16 = f32[2,128,128]{1,2,0:T(8,128)S(1)} custom-call(f32[2,128,128]{2,1,0:T(8,128)S(1)} %get-tuple-element.9), custom_call_target="InvertDiagBlocksLowerTriangular" | custom-call | tf_op jit(solution)/shard_map/jit(_solve_triangular)/triangular_solve | solution.py:14
  269.3 0.7 copy.9
  270.1 80.7 %all-gather.3.cloned.1.call-done = f32[2048,256]{1,0:T(8,128)} async-done(((f32[32,256]{1,0:T(8,128)}), f32[2048,256]{1,0:T(8,128)}) %all-gather.3.cloned.1.call-update) | async-done | bytes 2097168 | tf_op jit(solution)/shard_map/all_gather | solution.py:16
  350.7 4.2 convolution_bitcast_fusion
  355.0 71.6 %all-reduce.7.cloned.1.call-done = f32[256,256]{1,0:T(8,128)} async-done(((f32[256,256]{1,0:T(8,128)}), f32[256,256]{1,0:T(8,128)}) %all-reduce.7.cloned.1.call-update) | async-done | bytes 262160 | tf_op jit(solution)/shard_map/psum | solution.py:19
  426.6 2.0 fusion.2
  428.7 193.9 %all-reduce.9.cloned.1.call-done = f32[256,256]{1,0:T(8,128)} async-done(((f32[256,256]{1,0:T(8,128)}), f32[256,256]{1,0:T(8,128)}) %all-reduce.9.cloned.1.call-update) | async-done | bytes 262160 | tf_op jit(solution)/shard_map/psum | solution.py:20
  622.6 1.6 fusion
  624.2 0.6 constant_dynamic-slice_fusion.1
  624.9 82.1 %all-gather.5.cloned.1.call-done = f32[2048,256]{1,0:T(8,128)} async-done(((f32[32,256]{1,0:T(8,128)}), f32[2048,256]{1,0:T(8,128)}) %all-gather.5.cloned.1.call-update) | async-done | bytes 2097168 | tf_op jit(solution)/shard_map/all_gather | solution.py:23
  707.0 5.3 convolution_subtract_fusion.1
  712.3 3.4 convolution_subtract_fusion
  715.6 0.7 copy.26
  (36 shorter events, 3.3 us)
Async XLA Ops:
  7.2 199.3 %all-reduce.5.cloned.1.call-start = ((), (), s32[]{:S(2)}) async-start(), calls=%async_computation | async-start | bytes 524288 | tf_op jit(solution)/shard_map/psum | solution.py:12
  9.5 258.6 %copy-start.2 = (f32[256,256]{1,0:T(8,128)S(1)}, f32[256,256]{1,0:T(8,128)}, u32[]{:S(2)}) copy-start(f32[256,256]{1,0:T(8,128)} %param.2) | copy-start | bytes 786436
  9.6 341.1 %all-gather.3.cloned.1.call-start = ((), (), s32[]{:S(2)}) async-start(), calls=%async_computation.1 | async-start | bytes 2129920 | tf_op jit(solution)/shard_map/all_gather | solution.py:16
  220.2 130.5 %copy-start = (f32[256,2048]{1,0:T(8,128)S(1)}, f32[256,2048]{1,0:T(8,128)}, u32[]{:S(2)}) copy-start(f32[256,2048]{1,0:T(8,128)} %param.3) | copy-start | bytes 6291460
  270.0 156.6 %all-reduce.7.cloned.1.call-start = ((), (), s32[]{:S(2)}) async-start(), calls=%async_computation.2 | async-start | bytes 524288 | tf_op jit(solution)/shard_map/psum | solution.py:19
  355.0 267.6 %all-reduce.9.cloned.1.call-start = ((), (), s32[]{:S(2)}) async-start(), calls=%async_computation.3 | async-start | bytes 524288 | tf_op jit(solution)/shard_map/psum | solution.py:20
  428.7 278.3 %all-gather.5.cloned.1.call-start = ((), (), s32[]{:S(2)}) async-start(), calls=%async_computation.4 | async-start | bytes 2129920 | tf_op jit(solution)/shard_map/all_gather | solution.py:23
  707.0 5.3 copy-start.1
  712.2 3.4 copy-start.3
Sparse Core Ops, SparseCore 0:
  12.0 194.3 all-reduce.4
  270.1 80.5 all-gather.2
  355.1 71.4 all-reduce.6
  430.5 192.0 all-reduce.8
  626.4 80.5 all-gather.4
where the time goes:
time: 723 us
  waiting for transfers between devices  625 us (86%)
  other arithmetic  54.8 us (8%)
  matrix products  20.3 us (3%)
  between operations  15.2 us (2%)
    psum x1, waiting for transfers between devices, shards(): lax.psum(jnp.dot(panel_cols.T, panel_cols, precision=high), 'row')  197 us
    psum x1, waiting for transfers between devices, shards(): band_block = lax.psum(jnp.dot(ortho_basis.T, moment, precision=high), 'row')  194 us
    all_gather x1, waiting for transfers between devices, shards(): update_cols = lax.all_gather(own_corrected, 'row', axis=0, tiled=True)  82.1 us
    all_gather x1, waiting for transfers between devices, shards(): arrived = lax.all_gather(own_basis, 'row', axis=0, tiled=True)  80.7 us
    psum x1, waiting for transfers between devices, shards(): moment = lax.psum(partial_sum, 'col')  71.6 us
    another operation x6, other arithmetic, shards(): lower_factor = jnp.linalg.cholesky(gram_sum)  34 us
    another operation x3, other arithmetic, shards(): jax.scipy.linalg.solve_triangular(lower_factor, panel_cols.T, lower=True)  19.7 us
  transfers between devices with their start and end apart: 5, of which 5 were waited for; matrix products, arithmetic and copies ran while one was open for 0% of the time, Pallas kernels for 0%

commit v1 on v0

--- a/solution.py
+++ b/solution.py
@@ -2,6 +2,7 @@
 import jax.numpy as jnp
 from jax import lax
 from jax.sharding import PartitionSpec as P
+from jax.lax import all_gather
 
 
 def shards(panel_cols, affinity):
@@ -17,7 +18,8 @@
     partial_sum = jnp.dot(affinity, arrived, precision=high)
     partial_sum, basis_cols = (partial_sum, arrived)
     moment = lax.psum(partial_sum, "col")
-    band_block = lax.psum(jnp.dot(ortho_basis.T, moment, precision=high), "row")
+    z_in = jnp.dot(ortho_basis.T, moment, precision=high)
+    band_block = jnp.sum(all_gather(z_in, "row"), axis=0)
     corrected = moment - 0.5 * jnp.dot(ortho_basis, band_block, precision=high)
     own_corrected = lax.dynamic_slice_in_dim(corrected, col_place * piece_rows, piece_rows, 0)
     update_cols = lax.all_gather(own_corrected, "row", axis=0, tiled=True)

time: 723 us -> 642 us (0.89)
  waiting for transfers between devices: 625 us -> 539 us
    psum x1 -> x0, waiting for transfers between devices: 194 us -> none  [shards(): band_block = lax.psum(jnp.dot(ortho_basis.T, moment, precision=high), 'row')]
    all_gather x0 -> x1, waiting for transfers between devices: none -> 110 us  [shards(): band_block = jnp.sum(all_gather(z_in, 'row'), axis=0)]
where the time goes in v1:
time: 642 us
  waiting for transfers between devices  539 us (84%)
  other arithmetic  61.6 us (10%)
  matrix products  19.3 us (3%)
  between operations  15.2 us (2%)
    psum x1, waiting for transfers between devices, shards(): lax.psum(jnp.dot(panel_cols.T, panel_cols, precision=high), 'row')  197 us
    all_gather x1, waiting for transfers between devices, shards(): band_block = jnp.sum(all_gather(z_in, 'row'), axis=0)  110 us
    all_gather x1, waiting for transfers between devices, shards(): arrived = lax.all_gather(own_basis, 'row', axis=0, tiled=True)  80.7 us
    all_gather x1, waiting for transfers between devices, shards(): update_cols = lax.all_gather(own_corrected, 'row', axis=0, tiled=True)  80.3 us
    psum x1, waiting for transfers between devices, shards(): moment = lax.psum(partial_sum, 'col')  71.6 us
    another operation x6, other arithmetic, shards(): lower_factor = jnp.linalg.cholesky(gram_sum)  33.9 us
    another operation x3, other arithmetic, shards(): jax.scipy.linalg.solve_triangular(lower_factor, panel_cols.T, lower=True)  19.7 us
  transfers between devices with their start and end apart: 5, of which 5 were waited for; matrix products, arithmetic and copies ran while one was open for 0% of the time, Pallas kernels for 0%

profile of v1, /device:TPU:1, one launch (start us, length us, event | category | flops | bytes accessed | tf_op | source)
XLA Modules:
  0.0 641.8 jit_solution(11749878021910143240)
XLA Ops:
  7.2 2.4 fusion.16
  9.7 196.7 %all-reduce.4.cloned.1.call-done = f32[256,256]{0,1:T(8,128)} async-done(((f32[256,256]{0,1:T(8,128)}), f32[256,256]{0,1:T(8,128)}) %all-reduce.4.cloned.1.call-update) | async-done | bytes 262160 | tf_op jit(solution)/shard_map/psum | solution.py:13
  206.4 1.1 copy.8
  207.5 1.0 fusion.1
  208.5 11.7 %cholesky.50 = f32[128,128]{1,0:T(8,128)S(1)} custom-call(f32[128,128]{1,0:T(8,128)S(1)} %cholesky.118), custom_call_target="Cholesky" | custom-call | tf_op jit(solution)/shard_map/jit(cholesky)/cholesky | solution.py:14
  220.3 9.8 %custom-call.15 = f32[1,128,128]{1,2,0:T(8,128)S(1)} custom-call(f32[1,128,128]{2,1,0:T(8,128)S(1)} %get-tuple-element.23), custom_call_target="InvertDiagBlocksLowerTriangular" | custom-call | tf_op jit(solution)/shard_map/jit(cholesky)/cholesky | solution.py:14
  230.6 11.7 %cholesky.105 = f32[128,128]{1,0:T(8,128)S(1)} custom-call(f32[128,128]{1,0:T(8,128)S(1)} %convolution_subtract_fusion.3), custom_call_target="Cholesky" | custom-call | tf_op jit(solution)/shard_map/jit(cholesky)/cholesky | solution.py:14
  242.3 0.6 compare_reduce_fusion
  244.3 4.0 while.1
  245.0 1.3 bitcast_dynamic-update-slice_fusion.2
  247.0 1.3 bitcast_dynamic-update-slice_fusion.2
  248.3 19.7 %custom-call.16 = f32[2,128,128]{1,2,0:T(8,128)S(1)} custom-call(f32[2,128,128]{2,1,0:T(8,128)S(1)} %get-tuple-element.9), custom_call_target="InvertDiagBlocksLowerTriangular" | custom-call | tf_op jit(solution)/shard_map/jit(_solve_triangular)/triangular_solve | solution.py:15
  269.1 0.7 copy.9
  269.9 80.7 %all-gather.5.cloned.1.call-done = f32[2048,256]{1,0:T(8,128)} async-done(((f32[32,256]{1,0:T(8,128)}), f32[2048,256]{1,0:T(8,128)}) %all-gather.5.cloned.1.call-update) | async-done | bytes 2097168 | tf_op jit(solution)/shard_map/all_gather | solution.py:17
  350.5 4.2 convolution_bitcast_fusion
  354.8 71.6 %all-reduce.6.cloned.1.call-done = f32[256,256]{1,0:T(8,128)} async-done(((f32[256,256]{1,0:T(8,128)}), f32[256,256]{1,0:T(8,128)}) %all-reduce.6.cloned.1.call-update) | async-done | bytes 262160 | tf_op jit(solution)/shard_map/psum | solution.py:20
  426.4 2.0 fusion.2
  428.5 109.6 %all-gather.9.cloned.1.call-done = f32[16384,256]{1,0:T(8,128)} async-done(((f32[256,256]{1,0:T(8,128)}), f32[16384,256]{1,0:T(8,128)}) %all-gather.9.cloned.1.call-update) | async-done | bytes 16777232 | tf_op jit(solution)/shard_map/all_gather | solution.py:22
  538.1 6.9 %reduce_sum.9 = f32[256,256]{1,0:T(8,128)S(1)} reduce(f32[64,256,256]{2,1,0:T(8,128)} %bitcast.46, f32[]{:T(128)} %constant.83.clone.1), dimensions={0}, to_apply=%region_6.7 | reduce | flops 4128768 | bytes 17039364 | tf_op jit(solution)/shard_map/reduce_sum | solution.py:22
  545.0 0.6 fusion
  545.6 0.6 constant_dynamic-slice_fusion.1
  546.3 80.3 %all-gather.7.cloned.1.call-done = f32[2048,256]{1,0:T(8,128)} async-done(((f32[32,256]{1,0:T(8,128)}), f32[2048,256]{1,0:T(8,128)}) %all-gather.7.cloned.1.call-update) | async-done | bytes 2097168 | tf_op jit(solution)/shard_map/all_gather | solution.py:25
  626.6 5.3 convolution_subtract_fusion.1
  631.9 3.4 convolution_subtract_fusion
  (38 shorter events, 3.3 us)
Async XLA Ops:
  7.2 199.3 %all-reduce.4.cloned.1.call-start = ((), (), s32[]{:S(2)}) async-start(), calls=%async_computation | async-start | bytes 524288 | tf_op jit(solution)/shard_map/psum | solution.py:13
  9.6 258.4 %copy-start.2 = (f32[256,256]{1,0:T(8,128)S(1)}, f32[256,256]{1,0:T(8,128)}, u32[]{:S(2)}) copy-start(f32[256,256]{1,0:T(8,128)} %param.2) | copy-start | bytes 786436
  9.6 340.9 %all-gather.5.cloned.1.call-start = ((), (), s32[]{:S(2)}) async-start(), calls=%async_computation.1 | async-start | bytes 2129920 | tf_op jit(solution)/shard_map/all_gather | solution.py:17
  220.2 130.3 %copy-start = (f32[256,2048]{1,0:T(8,128)S(1)}, f32[256,2048]{1,0:T(8,128)}, u32[]{:S(2)}) copy-start(f32[256,2048]{1,0:T(8,128)} %param.3) | copy-start | bytes 6291460
  269.8 156.6 %all-reduce.6.cloned.1.call-start = ((), (), s32[]{:S(2)}) async-start(), calls=%async_computation.2 | async-start | bytes 524288 | tf_op jit(solution)/shard_map/psum | solution.py:20
  354.8 183.4 %all-gather.9.cloned.1.call-start = ((), (), s32[]{:S(2)}) async-start(), calls=%async_computation.4 | async-start | bytes 17039360 | tf_op jit(solution)/shard_map/all_gather | solution.py:22
  428.5 198.1 %all-gather.7.cloned.1.call-start = ((), (), s32[]{:S(2)}) async-start(), calls=%async_computation.3 | async-start | bytes 2129920 | tf_op jit(solution)/shard_map/all_gather | solution.py:25
  538.1 6.9 %copy-start.4 = (f32[256,256]{1,0:T(8,128)S(1)}, f32[256,256]{1,0:T(8,128)}, u32[]{:S(2)}) copy-start(f32[256,256]{1,0:T(8,128)} %all-reduce.6.cloned.1.call-done) | copy-start | bytes 786436
  545.0 86.8 %copy-start.3 = (f32[256,256]{1,0:T(8,128)}, f32[256,256]{1,0:T(8,128)S(1)}, u32[]{:S(2)}) copy-start(f32[256,256]{1,0:T(8,128)S(1)} %reduce_sum.9) | copy-start | bytes 786436
  626.6 5.3 copy-start.1
Sparse Core Ops, SparseCore 0:
  12.0 194.3 all-reduce.3
  269.9 80.5 all-gather.4
  354.9 71.4 all-reduce.5
  430.2 107.8 all-gather.8
  546.4 80.1 all-gather.6
